TPU v7x, 256 devices: a whole 4x4x8 slice. The times are simulated.
256 devices in a mesh: rep: 16 (over z, core), wide: 4 (over x), narrow: 4 (over y).
Axes of the slice: x: 4, y: 4, z: 8, core: 2. Of those that a mesh axis runs over, the one named last changes fastest.
Arguments:
- tokens: bfloat16 [16384, 1536], P(('rep', 'wide'), 'narrow'), parts along dimension 0, may hold values from -6 to 6
- attn_gain: float32 [1536], replicated, may hold values from 0.1 to 1.9
- w_qkv: bfloat16 [1536, 2048], P(None, ('wide', 'narrow')), may hold values from -0.15625 to 0.15625
- w_out: bfloat16 [1536, 1536], P(None, 'narrow'), may hold values from -0.15625 to 0.15625
- prefix_cache: bfloat16 [2, 32, 8192, 2, 128], P(None, 'rep', ('wide', 'narrow')), parts along dimension 1, may hold values from -1500 to 1500
- decode_cache: bfloat16 [2, 64, 8192, 2, 128], P(None, 'rep', ('wide', 'narrow')), parts along dimension 1, may hold values from -1500 to 1500
- offsets: int32 [32], P('rep'), parts along dimension 0, may hold values from 1 to 8192, as said below
- lengths: int32 [64], P('rep'), parts along dimension 0, may hold values from 1 to 8192, as said below
Outputs:
- mixed: bfloat16 [16384, 1536], P(('rep', 'wide'), 'narrow'), parts along dimension 0
There are 16 independent parts, one for each index of `rep`. A program takes and returns all parts, laid end to end along the dimension named above; an argument that names none is the same for every part. Nothing has to cross between parts.
Inputs may be any that keep to these rules, and one draw needn't show every extreme that they name: `offsets`: exactly one prefill block has 8192 cached positions. `lengths`: exactly one decode has 8192 cached positions.
All inputs are finite; a program needn't handle non-finite values.
Results may differ from a plain program's by a relative error of at most 0.008.
Values may be sent and summed in bfloat16 or wider, within the bound.
No kernel may reach another device: no remote copies, remote signals or barrier semaphores. Data moves between devices by JAX's collectives and lax.ppermute only.
A program may use at most 320 MiB of HBM per device.

v0:
```python
import jax
import jax.numpy as jnp
from jax import lax
from jax.sharding import PartitionSpec as P

EPS = 1e-06
NEG = -1e30


def normalize(rows, gain):
    full = rows.astype(jnp.float32)
    meansq = jnp.mean(full * full, -1, keepdims=True)
    return (full * lax.rsqrt(meansq + EPS) * gain).astype(jnp.bfloat16)


def partial_softmax(grouped_queries, keys, values, allowed, form_s, form_o):
    scores = jnp.einsum(
        form_s, grouped_queries, keys, preferred_element_type=jnp.float32
    ) * grouped_queries.shape[-1] ** (-0.5)
    masked = jnp.where(allowed, scores, NEG)
    peak = jnp.max(masked, -1)
    weights = jnp.where(allowed, jnp.exp(masked - peak[..., None]), 0.0)
    total = jnp.sum(weights, -1)
    weighted = jnp.einsum(
        form_o, weights.astype(jnp.bfloat16), values, preferred_element_type=jnp.float32
    )
    return (peak, total, weighted)


def join_parts(first, second):
    peak = jnp.maximum(first[0], second[0])
    scale_a = jnp.exp(first[0] - peak)
    scale_b = jnp.exp(second[0] - peak)
    total = first[1] * scale_a + second[1] * scale_b
    weighted = first[2] * heads_major(scale_a) + second[2] * heads_major(scale_b)
    return (peak, total, weighted)


def heads_major(scale):
    return scale.transpose(1, 2, 0)[..., None]


def per_device(tokens, attn_gain, w_qkv, w_out, prefix_cache, decode_cache, offsets, lengths):
    n_wide = lax.axis_size("wide")
    n_narrow = lax.axis_size("narrow")
    devices = n_wide * n_narrow
    joined = lax.axis_index("wide") * n_narrow + lax.axis_index("narrow")
    block_rows = tokens.shape[0]
    every_rows = block_rows * n_wide
    own = every_rows // devices
    head_dim = prefix_cache.shape[-1]
    kv_heads = prefix_cache.shape[-2]
    n_prefix = prefix_cache.shape[1]
    n_decode = decode_cache.shape[1]
    span = (every_rows - n_decode) // n_prefix
    q_width = w_out.shape[0]
    heads = q_width // head_dim
    group = heads // kv_heads
    starts = (offsets[:, None] + jnp.arange(span, dtype=jnp.int32)[None, :]).reshape(-1)
    positions = jnp.concatenate([starts, lengths])
    row_ids = jnp.arange(every_rows, dtype=jnp.int32)
    sequence = jnp.where(
        row_ids < n_prefix * span, row_ids // span, row_ids - n_prefix * span + n_prefix
    )
    own_start = joined * own
    own_pos = lax.dynamic_slice_in_dim(positions, own_start, own)
    own_seq = lax.dynamic_slice_in_dim(sequence, own_start, own)
    features = lax.all_gather(tokens, "narrow", axis=1, tiled=True)
    normed_rows = normalize(features, attn_gain)
    w_cols = lax.all_gather(w_qkv, "wide", axis=0, tiled=False)
    part = jnp.einsum(
        "rf,wfc->rwc", normed_rows, w_cols, preferred_element_type=jnp.float32
    ).astype(jnp.bfloat16)
    col_block = w_qkv.shape[1]
    q_blocks = q_width // (n_narrow * col_block)
    gathered = lax.all_gather(part[:, :q_blocks], ("wide", "narrow"), axis=0, tiled=False)
    query_matrix = (
        gathered.reshape(n_wide, n_narrow, block_rows, q_blocks, col_block)
        .transpose(0, 2, 3, 1, 4)
        .reshape(every_rows, heads, head_dim)
    )
    fresh_kv = part[:, q_blocks:].reshape(n_narrow, own, col_block)
    fresh_kv = lax.all_to_all(fresh_kv, "narrow", 0, 0)
    own_keys = fresh_kv[:kv_heads].transpose(1, 0, 2)
    own_values = fresh_kv[kv_heads:].transpose(1, 0, 2)
    grouped_queries = query_matrix.reshape(every_rows, kv_heads, group, head_dim)
    shard = prefix_cache.shape[2]
    cache_pos = joined * shard + jnp.arange(shard, dtype=jnp.int32)
    pieces = []
    for index in range(n_prefix):
        block = grouped_queries[index * span : (index + 1) * span]
        allowed = (cache_pos < offsets[index])[None, None, None, :]
        pieces.append(
            partial_softmax(
                block,
                prefix_cache[0, index],
                prefix_cache[1, index],
                allowed,
                "qhgd,khd->qhgk",
                "qhgk,khd->hgqd",
            )
        )
    allowed = (cache_pos[None, :] < lengths[:, None])[:, None, None, :]
    pieces.append(
        partial_softmax(
            grouped_queries[n_prefix * span :],
            decode_cache[0],
            decode_cache[1],
            allowed,
            "nhgd,nkhd->nhgk",
            "nhgk,nkhd->hgnd",
        )
    )
    cached = tuple(
        (jnp.concatenate([piece[slot] for piece in pieces], 2 * (slot // 2)) for slot in range(3))
    )
    allowed = ((sequence[:, None] == own_seq[None, :]) & (own_pos[None, :] <= positions[:, None]))[
        :, None, None, :
    ]
    fresh = partial_softmax(
        grouped_queries, own_keys, own_values, allowed, "rhgd,khd->rhgk", "rhgk,khd->hgrd"
    )
    peak, total, weighted = join_parts(cached, fresh)
    top = lax.pmax(peak, "narrow")
    hi = lax.reduce_precision(top, exponent_bits=8, mantissa_bits=7)
    lo = lax.reduce_precision(top - hi, exponent_bits=8, mantissa_bits=7)
    shift = hi + lo
    scale = jnp.exp(jnp.minimum(peak - shift, 80.0))
    first = lax.axis_index("narrow") == 0

    def kept(a):
        return jnp.where(first, a, jnp.zeros_like(a)).reshape(every_rows, heads)

    lanes = 128
    extra = jnp.concatenate(
        [
            (total * scale).reshape(every_rows, heads),
            kept(hi),
            kept(lo),
            jnp.zeros((every_rows, lanes - 3 * heads), jnp.float32),
        ],
        1,
    )
    scaled = (weighted * heads_major(scale)).reshape(heads, every_rows, head_dim)
    packed = jnp.concatenate([scaled, extra[None]], 0).astype(jnp.bfloat16)
    slots = packed.shape[0]
    packed = (
        packed.reshape(slots, n_wide, n_narrow, own, head_dim)
        .transpose(0, 2, 1, 3, 4)
        .reshape(slots, every_rows, head_dim)
    )
    packed = lax.psum_scatter(packed, "narrow", scatter_dimension=1, tiled=True)
    packed = lax.all_to_all(packed.reshape(slots, n_wide, own, head_dim), "wide", 1, 1)
    packed = packed.astype(jnp.float32)
    extra = packed[heads]
    part_shift = extra[..., heads : 2 * heads] + extra[..., 2 * heads : 3 * heads]
    part_scale = jnp.exp(part_shift - jnp.max(part_shift, 0)[None])
    total = jnp.sum(extra[..., :heads] * part_scale, 0)
    weighted = jnp.sum(packed[:heads] * part_scale.transpose(2, 0, 1)[..., None], 1)
    attended = weighted / total.T[..., None]
    attended = attended.astype(jnp.bfloat16).transpose(1, 0, 2).reshape(own, q_width)
    mine_rows = lax.all_gather(attended, "narrow", axis=0, tiled=True)
    mixed = tokens.astype(jnp.float32) + jnp.dot(
        mine_rows, w_out, preferred_element_type=jnp.float32
    )
    return mixed.astype(jnp.bfloat16)


def solution(mesh):
    return jax.shard_map(
        per_device,
        mesh=mesh,
        in_specs=(
            P(("rep", "wide"), "narrow"),
            P(),
            P(None, ("wide", "narrow")),
            P(None, "narrow"),
            P(None, "rep", ("wide", "narrow"), None, None),
            P(None, "rep", ("wide", "narrow"), None, None),
            P("rep"),
            P("rep"),
        ),
        out_specs=P(("rep", "wide"), "narrow"),
        check_vma=False,
    )
```

profile of v0, /device:TPU:32, one launch (start us, length us, event | category | flops | bytes accessed | tf_op | source)
XLA Modules:
  0.0 237.3 jit_solution(5814794510141817188)
XLA Ops:
  6.6 0.7 all-gather.5.cloned.1.call-update
  7.3 14.8 %all_gather.18 = bf16[256,1536]{1,0:T(8,128)(2,1)S(1)} all-gather(bf16[256,384]{1,0:T(8,128)(2,1)} %param.8), channel_id=1, replica_groups=mesh['rep'=16,'wide'=4,'narrow'=4] {'narrow'}, dimensions={1}, use_global_device_ids=true | all-gather | bytes 983040 | tf_op jit(solution)/shard_map/all_gather | solution.py:68
  22.4 18.4 %all-gather.5.cloned.1.call-done = bf16[6144,128]{1,0:T(8,128)(2,1)} async-done(((bf16[1536,128]{1,0:T(8,128)(2,1)}), bf16[6144,128]{1,0:T(8,128)(2,1)}) %all-gather.5.cloned.1.call-update) | async-done | bytes 1572880 | tf_op jit(solution)/shard_map/all_gather | solution.py:70
  40.8 2.0 convolution_convert_fusion
  42.8 0.7 copy-done.7
  43.5 0.7 slice.80
  44.7 0.7 fusion.93
  45.4 1.3 fusion.76
  46.7 0.7 compare_and_fusion
  47.5 1.5 fusion.92
  49.0 1.5 fusion.91
  50.5 1.5 slice.84
  52.0 4.3 %all-to-all-start = ((bf16[4,64,128]{2,1,0:T(8,128)(2,1)}), bf16[4,64,128]{2,1,0:T(8,128)(2,1)}, u32[]{:S(2)}, u32[]{:S(2)}) async-start(bf16[4,64,128]{2,1,0:T(8,128)(2,1)} %bitcast.160), calls=%async_computation | async-start | bytes 131072 | tf_op jit(solution)/shard_map/all_to_all | solution.py:83
  56.3 41.0 %all-gather.7.cloned.1.call-done = bf16[4096,3,128]{2,0,1:T(8,128)(2,1)} async-done(((bf16[256,3,128]{2,0,1:T(8,128)(2,1)}), bf16[4096,3,128]{2,0,1:T(8,128)(2,1)}) %all-gather.7.cloned.1.call-update) | async-done | bytes 3145744 | tf_op jit(solution)/shard_map/all_gather | solution.py:76
  97.3 2.3 copy.85
  100.4 1.9 bitcast_reduce_fusion
  102.3 3.6 %fusion.6 = f32[510,2,6]{0,2,1:T(8,128)S(1)} fusion(f32[2,510,6,512]{3,1,2,0:T(8,128)S(1)} %get-tuple-element.27, f32[510,2,6]{0,2,1:T(8,128)S(1)} %get-tuple-element.26, pred[512]{0:T(512)(128)(4,1)S(1)} %get-tuple-element.32), kind=kLoop, calls=%fused_computation.12 | loop fusion | flops 15661080 | bytes 12583232 | tf_op jit(solution)/shard_map/reduce_sum | solution.py:23
  105.9 4.2 %fusion.25 = f32[2,6,510,128]{3,2,1,0:T(8,128)} fusion(f32[2,510,6,512]{3,1,2,0:T(8,128)S(1)} %get-tuple-element.27, f32[510,2,6]{0,2,1:T(8,128)S(1)} %get-tuple-element.26, pred[512]{0:T(512)(128)(4,1)S(1)} %get-tuple-element.32, bf16[1,1,512,2,128]{4,3,2,1,0:T(2,128)(2,1)S(1)} %copy-done.9), kind=kOutput, calls=%fused_computation.34 | convolution fusion | flops 817827840 | bytes 15954336 | tf_op jit(solution)/shard_map/qhgk,khd->hgqd/dot_general | solution.py:24
  110.4 3.3 %fusion.19 = (f32[1024,2,6]{0,2,1:T(8,128)S(1)}, f32[2,64,1024,6]{2,1,3,0:T(8,128)S(1)}) fusion(pred[1024,64]{0,1:T(8,128)(4,1)S(1)} %copy-done.5, bf16[1024,2,6,128]{3,0,2,1:T(8,128)(2,1)} %bitcast.154, bf16[4,64,128]{2,1,0:T(8,128)(2,1)} %all-to-all-done), kind=kOutput, calls=%fused_computation.28 | convolution fusion | flops 203673600 | bytes 6438912 | tf_op jit(solution)/shard_map/rhgd,khd->rhgk/dot_general | solution.py:17
  113.7 0.8 fusion.20
  114.5 0.8 copy-done.3
  115.4 1.9 bitcast_reduce_fusion.1
  117.4 3.6 %fusion.4 = f32[510,2,6]{0,2,1:T(8,128)S(1)} fusion(f32[2,510,6,512]{3,1,2,0:T(8,128)S(1)} %get-tuple-element.29, f32[510,2,6]{0,2,1:T(8,128)S(1)} %get-tuple-element.28, pred[512]{0:T(512)(128)(4,1)S(1)} %get-tuple-element.33), kind=kLoop, calls=%fused_computation.10 | loop fusion | flops 15661080 | bytes 12583232 | tf_op jit(solution)/shard_map/reduce_sum | solution.py:23
  121.0 4.2 %fusion.22 = f32[2,6,510,128]{3,2,1,0:T(8,128)} fusion(f32[2,510,6,512]{3,1,2,0:T(8,128)S(1)} %get-tuple-element.29, f32[510,2,6]{0,2,1:T(8,128)S(1)} %get-tuple-element.28, pred[512]{0:T(512)(128)(4,1)S(1)} %get-tuple-element.33, bf16[1,1,512,2,128]{4,3,2,1,0:T(2,128)(2,1)S(1)} %copy-done.8), kind=kOutput, calls=%fused_computation.33 | convolution fusion | flops 817827840 | bytes 15954336 | tf_op jit(solution)/shard_map/qhgk,khd->hgqd/dot_general | solution.py:24
  125.2 16.5 %pmax.7 = f32[1024,2,6]{0,2,1:T(8,128)S(1)} all-reduce(f32[1024,2,6]{0,2,1:T(8,128)S(1)} %get-tuple-element.6), channel_id=1, replica_groups=mesh['rep'=16,'wide'=4,'narrow'=4] {'narrow'}, use_global_device_ids=true, to_apply=%region_5.6 | all-reduce | flops 12288 | bytes 98304 | tf_op jit(solution)/shard_map/pmax | solution.py:124
  142.8 8.7 %fusion.10 = bf16[2,6,1024,128]{3,2,1,0:T(8,128)(2,1)S(1)} fusion(f32[2,6,4,128]{3,2,1,0:T(4,128)S(1)} %bitcast.161, f32[2,6,510,128]{3,2,1,0:T(8,128)} %fusion.25, f32[2,6,510,128]{3,2,1,0:T(8,128)} %fusion.22, f32[2,6,1024]{2,1,0:T(8,128)S(1)} %get-tuple-element.19, f32[2,6,1024]{2,1,0:T(8,128)S(1)} %get-tuple-element.17, ...), kind=kOutput, calls=%fused_computation.17 | convolution fusion | flops 216268800 | bytes 12902400 | tf_op jit(solution)/shard_map/rhgk,khd->hgrd/dot_general | solution.py:24
  151.4 3.3 %maximum_maximum_fusion = bf16[13,4,4,64,128]{4,3,1,2,0:T(8,128)(2,1)} fusion(bf16[1,4,4,64,12]{4,3,1,2,0:T(8,128)(2,1)S(1)} %copy.104, bf16[1,4,4,64,12]{4,3,1,2,0:T(8,128)(2,1)S(1)} %copy.103, bf16[1,4,4,64,12]{4,3,1,2,0:T(8,128)(2,1)S(1)} %copy.102, bf16[13,128]{1,0:T(8,128)(2,1)S(1)} %pad.4.clone, bf16[12,4,4,64,128]{4,3,2,1,0:T(8,128)(2,1)S(1)} %bitcast.158), kind=kLoop, calls=%fused_computation.25 | loop fusion | flops 17039360 | bytes 6630656 | tf_op jit(solution)/shard_map/concatenate | solution.py:145
  154.7 41.7 %reduce-scatter.2.cloned.1.call-done = bf16[13,256,128]{2,1,0:T(8,128)(2,1)} async-done(((bf16[13,1024,128]{2,1,0:T(8,128)(2,1)}), bf16[13,256,128]{2,1,0:T(8,128)(2,1)}) %reduce-scatter.2.cloned.1.call-update) | async-done | bytes 851984 | tf_op jit(solution)/shard_map/reduce_scatter | solution.py:152
  196.4 1.2 copy.106
  197.7 17.0 %all_to_all.10 = bf16[13,4,64,128]{3,2,0,1:T(8,128)(2,1)S(1)} all-to-all(bf16[13,4,64,128]{3,2,0,1:T(8,128)(2,1)S(1)} %copy.106), channel_id=1, replica_groups=mesh['rep'=16,'wide'=4,'narrow'=4] {'wide'}, dimensions={1} | all-to-all | bytes 1703936 | tf_op jit(solution)/shard_map/all_to_all | solution.py:153
  216.0 13.5 %all_gather.23 = bf16[256,1536]{1,0:T(8,128)(2,1)S(1)} all-gather(bf16[64,1536]{1,0:T(8,128)(2,1)S(1)} %copy_bitcast_fusion.12), channel_id=1, replica_groups=mesh['rep'=16,'wide'=4,'narrow'=4] {'narrow'}, dimensions={0}, use_global_device_ids=true | all-gather | bytes 983040 | tf_op jit(solution)/shard_map/all_gather | solution.py:162
  229.5 1.3 fusion.42
  (65 shorter events, 4.4 us)
Async XLA Ops:
  6.5 222.9 %copy-start = (bf16[1536,384]{1,0:T(8,128)(2,1)S(1)}, bf16[1536,384]{1,0:T(8,128)(2,1)}, u32[]{:S(2)}) copy-start(bf16[1536,384]{1,0:T(8,128)(2,1)} %param.11) | copy-start | bytes 3538948
  6.5 37.7 %copy-start.12 = (s32[2]{0:T(128)S(1)}, s32[2]{0:T(128)}, u32[]{:S(2)}) copy-start(s32[2]{0:T(128)} %param.14) | copy-start | bytes 28
  6.5 37.9 %copy-start.13 = (s32[4]{0:T(128)S(1)}, s32[4]{0:T(128)}, u32[]{:S(2)}) copy-start(s32[4]{0:T(128)} %param.15) | copy-start | bytes 52
  6.5 40.9 %copy-start.6 = (bf16[2,2,512,2,128]{4,3,2,1,0:T(2,128)(2,1)S(1)}, bf16[2,2,512,2,128]{4,3,2,1,0:T(2,128)(2,1)}, u32[]{:S(2)}) copy-start(bf16[2,2,512,2,128]{4,3,2,1,0:T(2,128)(2,1)} %param.12) | copy-start | bytes 3145732
  6.5 34.2 %all-gather.5.cloned.1.call-start = ((), (), s32[]{:S(2)}) async-start(), calls=%async_computation.4 | async-start | bytes 1966080 | tf_op jit(solution)/shard_map/all_gather | solution.py:70
  7.3 90.0 %all-gather.7.cloned.1.call-start = ((), (), s32[]{:S(2)}) async-start(), calls=%async_computation.5 | async-start | bytes 3342336 | tf_op jit(solution)/shard_map/all_gather | solution.py:76
  42.8 0.7 copy-start.7
  44.4 4.6 %copy-start.4 = (bf16[2,4,512,2,128]{4,3,2,1,0:T(2,128)(2,1)S(1)}, bf16[2,4,512,2,128]{4,3,2,1,0:T(2,128)(2,1)}, u32[]{:S(2)}) copy-start(bf16[2,4,512,2,128]{4,3,2,1,0:T(2,128)(2,1)} %param.13) | copy-start | bytes 6291460
  52.0 58.4 %all-to-all-start = ((bf16[4,64,128]{2,1,0:T(8,128)(2,1)}), bf16[4,64,128]{2,1,0:T(8,128)(2,1)}, u32[]{:S(2)}, u32[]{:S(2)}) async-start(bf16[4,64,128]{2,1,0:T(8,128)(2,1)} %bitcast.160), calls=%async_computation | async-start | bytes 131072 | tf_op jit(solution)/shard_map/all_to_all | solution.py:83
  56.3 140.2 %reduce-scatter.2.cloned.1.call-start = ((), (), s32[]{:S(2)}) async-start(), calls=%async_computation.3 | async-start | bytes 4259840 | tf_op jit(solution)/shard_map/reduce_scatter | solution.py:152
  97.3 3.1 %copy-start.10 = (bf16[1,1,512,2,128]{4,3,2,1,0:T(2,128)(2,1)S(1)}, bf16[1,1,512,2,128]{4,3,2,1,0:T(2,128)(2,1)}, u32[]{:S(2)}) copy-start(bf16[1,1,512,2,128]{4,3,2,1,0:T(2,128)(2,1)} %get-tuple-element.10) | copy-start | bytes 786436
  99.6 2.7 %copy-start.1 = (bf16[4,256,3,4,128]{4,1,0,3,2:T(8,128)(2,1)}, bf16[4,256,3,4,128]{4,1,0,3,2:T(8,128)(2,1)S(1)}, u32[]{:S(2)}) copy-start(bf16[4,256,3,4,128]{4,1,0,3,2:T(8,128)(2,1)S(1)} %copy.85) | copy-start | bytes 9437188
  102.3 3.6 %copy-start.9 = (bf16[1,1,512,2,128]{4,3,2,1,0:T(2,128)(2,1)S(1)}, bf16[1,1,512,2,128]{4,3,2,1,0:T(2,128)(2,1)}, u32[]{:S(2)}) copy-start(bf16[1,1,512,2,128]{4,3,2,1,0:T(2,128)(2,1)} %get-tuple-element.12) | copy-start | bytes 786436
  105.9 4.5 %copy-start.5 = (pred[1024,64]{0,1:T(8,128)(4,1)S(1)}, pred[1024,64]{0,1:T(8,128)(4,1)}, u32[]{:S(2)}) copy-start(pred[1024,64]{0,1:T(8,128)(4,1)} %compare_and_fusion) | copy-start | bytes 196612
  110.4 5.0 %copy-start.2 = (bf16[4,256,3,4,128]{4,1,0,3,2:T(8,128)(2,1)S(1)}, bf16[4,256,3,4,128]{4,1,0,3,2:T(8,128)(2,1)}, u32[]{:S(2)}) copy-start(bf16[4,256,3,4,128]{4,1,0,3,2:T(8,128)(2,1)} %copy-done.1) | copy-start | bytes 9437188
  113.7 1.7 copy-start.3
  117.4 3.6 %copy-start.8 = (bf16[1,1,512,2,128]{4,3,2,1,0:T(2,128)(2,1)S(1)}, bf16[1,1,512,2,128]{4,3,2,1,0:T(2,128)(2,1)}, u32[]{:S(2)}) copy-start(bf16[1,1,512,2,128]{4,3,2,1,0:T(2,128)(2,1)} %get-tuple-element.9) | copy-start | bytes 786436
  214.6 14.8 %copy-start.11 = (bf16[256,384]{1,0:T(8,128)(2,1)S(1)}, bf16[256,384]{1,0:T(8,128)(2,1)}, u32[]{:S(2)}) copy-start(bf16[256,384]{1,0:T(8,128)(2,1)} %param.8) | copy-start | bytes 589828
Sparse Core Ops, SparseCore 0:
  9.2 31.5 all-gather.4
  44.4 52.8 all-gather.6
  154.8 41.5 reduce-scatter.1
where the time goes:
time: 238 us; the launch traced here: 237 us
  waiting for transfers between devices  102 us (43%)
  blocking collectives  61.7 us (26%)
  matrix products  28.1 us (12%)
  other arithmetic  15.4 us (6%)
  between operations  13.4 us (6%)
  local copies, waits for them, and re-layouts  12.4 us (5%)
  starting transfers between devices  4.37 us (2%)
    reduce_scatter x1, waiting for transfers between devices, per_device(): packed = lax.psum_scatter(packed, 'narrow', scatter_dimension=1, tiled=True)  41.7 us
    all_gather x1, waiting for transfers between devices, per_device(): lax.all_gather(part[:, :q_blocks], ('wide', 'narrow'), axis=0, tiled=False)  41 us
    all_gather x1, waiting for transfers between devices, per_device(): w_cols = lax.all_gather(w_qkv, 'wide', axis=0, tiled=False)  18.4 us
    dot_general x4, matrix products, partial_softmax(): jnp.einsum(form_o, weights.astype(jnp.bfloat16), values, preferred_elemen...  17.4 us
    all_to_all x1, blocking collectives, per_device(): lax.all_to_all(packed.reshape(slots, n_wide, own, head_dim), 'wide', 1, 1)  17 us
    pmax x1, blocking collectives, per_device(): top = lax.pmax(peak, 'narrow')  16.5 us
    all_gather x1, blocking collectives, per_device(): features = lax.all_gather(tokens, 'narrow', axis=1, tiled=True)  14.8 us
    all_gather x1, blocking collectives, per_device(): mine_rows = lax.all_gather(attended, 'narrow', axis=0, tiled=True)  13.5 us
  transfers between devices with their start and end apart: 4, of which 3 were waited for; matrix products, arithmetic and copies ran while one was open for 9% of the time, Pallas kernels for 0%

commit v1 on v0

--- a/solution.py
+++ b/solution.py
@@ -65,7 +65,11 @@
     own_start = joined * own
     own_pos = lax.dynamic_slice_in_dim(positions, own_start, own)
     own_seq = lax.dynamic_slice_in_dim(sequence, own_start, own)
-    features = lax.all_gather(tokens, "narrow", axis=1, tiled=True)
+    size = lax.axis_size("narrow")
+    repeats = [size if d == 1 else 1 for d in range(tokens.ndim)]
+    features = lax.all_to_all(
+        jnp.tile(tokens, repeats), "narrow", split_axis=1, concat_axis=1, tiled=True
+    )
     normed_rows = normalize(features, attn_gain)
     w_cols = lax.all_gather(w_qkv, "wide", axis=0, tiled=False)
     part = jnp.einsum(

time: 238 us -> 238 us (level)
  waiting for transfers between devices: 102 us -> 96.8 us
  local copies, waits for them, and re-layouts: 12.4 us -> 14.9 us
    all_to_all x0 -> x1, blocking collectives: none -> 16.6 us  [per_device(): lax.all_to_all(jnp.tile(tokens, repeats), 'narrow', split_axis=1, concat_...]
    all_gather x1 -> x0, blocking collectives: 14.8 us -> none  [per_device(): features = lax.all_gather(tokens, 'narrow', axis=1, tiled=True)]
    all_gather x1, waiting for transfers between devices: 18.4 us -> 14.2 us  [per_device(): w_cols = lax.all_gather(w_qkv, 'wide', axis=0, tiled=False)]
  transfers between devices with their start and end apart: 4 -> 4, of which waited for: 3 -> 3; matrix products, arithmetic and copies ran while one was open for 9% -> 10% of each run, Pallas kernels for 0% -> 0%
where the time goes in v1:
time: 238 us
  waiting for transfers between devices  96.8 us (41%)
  blocking collectives  63.5 us (27%)
  matrix products  28.3 us (12%)
  other arithmetic  16.6 us (7%)
  local copies, waits for them, and re-layouts  14.9 us (6%)
  between operations  13.4 us (6%)
  starting transfers between devices  4.32 us (2%)
    reduce_scatter x1, waiting for transfers between devices, per_device(): packed = lax.psum_scatter(packed, 'narrow', scatter_dimension=1, tiled=True)  41.7 us
    all_gather x1, waiting for transfers between devices, per_device(): lax.all_gather(part[:, :q_blocks], ('wide', 'narrow'), axis=0, tiled=False)  40.1 us
    dot_general x4, matrix products, partial_softmax(): jnp.einsum(form_o, weights.astype(jnp.bfloat16), values, preferred_elemen...  17.4 us
    all_to_all x1, blocking collectives, per_device(): lax.all_to_all(packed.reshape(slots, n_wide, own, head_dim), 'wide', 1, 1)  17 us
    all_to_all x1, blocking collectives, per_device(): lax.all_to_all(jnp.tile(tokens, repeats), 'narrow', split_axis=1, concat_...  16.6 us
    pmax x1, blocking collectives, per_device(): top = lax.pmax(peak, 'narrow')  16.5 us
    all_gather x1, waiting for transfers between devices, per_device(): w_cols = lax.all_gather(w_qkv, 'wide', axis=0, tiled=False)  14.2 us
    all_gather x1, blocking collectives, per_device(): mine_rows = lax.all_gather(attended, 'narrow', axis=0, tiled=True)  13.5 us
  transfers between devices with their start and end apart: 4, of which 3 were waited for; matrix products, arithmetic and copies ran while one was open for 10% of the time, Pallas kernels for 0%

profile of v1, /device:TPU:32, one launch (start us, length us, event | category | flops | bytes accessed | tf_op | source)
XLA Modules:
  0.0 237.8 jit_solution(764749093044653207)
XLA Ops:
  6.5 0.7 all-gather.5.cloned.1.call-update
  7.3 1.0 tile.2
  8.3 16.6 %all_to_all.16 = bf16[256,4,384]{2,0,1:T(8,128)(2,1)S(1)} all-to-all(bf16[256,4,384]{2,0,1:T(8,128)(2,1)S(1)} %tile.2), channel_id=1, replica_groups=mesh['rep'=16,'wide'=4,'narrow'=4] {'narrow'}, dimensions={1} | all-to-all | bytes 1572864 | tf_op jit(solution)/shard_map/all_to_all | solution.py:70
  25.4 1.2 fusion.35
  26.6 14.2 %all-gather.5.cloned.1.call-done = bf16[6144,128]{1,0:T(8,128)(2,1)} async-done(((bf16[1536,128]{1,0:T(8,128)(2,1)}), bf16[6144,128]{1,0:T(8,128)(2,1)}) %all-gather.5.cloned.1.call-update) | async-done | bytes 1572880 | tf_op jit(solution)/shard_map/all_gather | solution.py:74
  40.8 2.2 convolution_convert_fusion
  43.0 0.7 copy-done.6
  45.6 1.3 fusion.72
  46.9 0.7 compare_and_fusion
  47.7 1.5 fusion.88
  49.2 2.7 %fusion.87 = (bf16[1,4,512,2,128]{4,3,2,1,0:T(2,128)(2,1)S(1)}, bf16[1,4,512,2,128]{4,3,2,1,0:T(2,128)(2,1)S(1)}) fusion(bf16[2,4,512,2,128]{4,3,2,1,0:T(2,128)(2,1)} %param.13), kind=kLoop, calls=%fused_computation.131 | loop fusion | bytes 4194304 | tf_op jit(solution)/shard_map/slice | solution.py:112
  51.9 1.5 slice.84
  53.4 4.3 %all-to-all-start.1 = ((bf16[4,64,128]{2,1,0:T(8,128)(2,1)}), bf16[4,64,128]{2,1,0:T(8,128)(2,1)}, u32[]{:S(2)}, u32[]{:S(2)}) async-start(bf16[4,64,128]{2,1,0:T(8,128)(2,1)} %bitcast.166), calls=%async_computation.1 | async-start | bytes 131072 | tf_op jit(solution)/shard_map/all_to_all | solution.py:87
  57.7 40.1 %all-gather.7.cloned.1.call-done = bf16[4096,3,128]{2,0,1:T(8,128)(2,1)} async-done(((bf16[256,3,128]{2,0,1:T(8,128)(2,1)}), bf16[4096,3,128]{2,0,1:T(8,128)(2,1)}) %all-gather.7.cloned.1.call-update) | async-done | bytes 3145744 | tf_op jit(solution)/shard_map/all_gather | solution.py:80
  97.8 2.3 copy.112
  100.8 1.9 bitcast_reduce_fusion
  102.8 3.6 %fusion.6 = f32[510,2,6]{0,2,1:T(8,128)S(1)} fusion(f32[2,510,6,512]{3,1,2,0:T(8,128)S(1)} %get-tuple-element.27, f32[510,2,6]{0,2,1:T(8,128)S(1)} %get-tuple-element.26, pred[512]{0:T(512)(128)(4,1)S(1)} %get-tuple-element.32), kind=kLoop, calls=%fused_computation.12 | loop fusion | flops 15661080 | bytes 12583232 | tf_op jit(solution)/shard_map/reduce_sum | solution.py:23
  106.3 4.2 %fusion.25 = f32[2,6,510,128]{3,2,1,0:T(8,128)} fusion(f32[2,510,6,512]{3,1,2,0:T(8,128)S(1)} %get-tuple-element.27, f32[510,2,6]{0,2,1:T(8,128)S(1)} %get-tuple-element.26, pred[512]{0:T(512)(128)(4,1)S(1)} %get-tuple-element.32, bf16[1,1,512,2,128]{4,3,2,1,0:T(2,128)(2,1)S(1)} %copy-done.8), kind=kOutput, calls=%fused_computation.32 | convolution fusion | flops 817827840 | bytes 15954336 | tf_op jit(solution)/shard_map/qhgk,khd->hgqd/dot_general | solution.py:24
  110.9 3.3 %fusion.19 = (f32[1024,2,6]{0,2,1:T(8,128)S(1)}, f32[2,64,1024,6]{2,1,3,0:T(8,128)S(1)}) fusion(pred[1024,64]{0,1:T(8,128)(4,1)S(1)} %copy-done.4, bf16[1024,2,6,128]{3,0,2,1:T(8,128)(2,1)} %bitcast.160, bf16[4,64,128]{2,1,0:T(8,128)(2,1)} %all-to-all-done.1), kind=kOutput, calls=%fused_computation.28 | convolution fusion | flops 203673600 | bytes 6438912 | tf_op jit(solution)/shard_map/rhgd,khd->rhgk/dot_general | solution.py:17
  114.2 0.8 fusion.20
  115.0 0.8 copy-done.3
  115.9 1.9 bitcast_reduce_fusion.1
  117.9 3.6 %fusion.4 = f32[510,2,6]{0,2,1:T(8,128)S(1)} fusion(f32[2,510,6,512]{3,1,2,0:T(8,128)S(1)} %get-tuple-element.29, f32[510,2,6]{0,2,1:T(8,128)S(1)} %get-tuple-element.28, pred[512]{0:T(512)(128)(4,1)S(1)} %get-tuple-element.33), kind=kLoop, calls=%fused_computation.10 | loop fusion | flops 15661080 | bytes 12583232 | tf_op jit(solution)/shard_map/reduce_sum | solution.py:23
  121.4 4.3 %fusion.22 = f32[2,6,510,128]{3,2,1,0:T(8,128)} fusion(f32[2,510,6,512]{3,1,2,0:T(8,128)S(1)} %get-tuple-element.29, f32[510,2,6]{0,2,1:T(8,128)S(1)} %get-tuple-element.28, pred[512]{0:T(512)(128)(4,1)S(1)} %get-tuple-element.33, bf16[1,1,512,2,128]{4,3,2,1,0:T(2,128)(2,1)S(1)} %copy-done.7), kind=kOutput, calls=%fused_computation.31 | convolution fusion | flops 817827840 | bytes 15954336 | tf_op jit(solution)/shard_map/qhgk,khd->hgqd/dot_general | solution.py:24
  125.7 16.5 %pmax.7 = f32[1024,2,6]{0,2,1:T(8,128)S(1)} all-reduce(f32[1024,2,6]{0,2,1:T(8,128)S(1)} %get-tuple-element.6), channel_id=1, replica_groups=mesh['rep'=16,'wide'=4,'narrow'=4] {'narrow'}, use_global_device_ids=true, to_apply=%region_5.6 | all-reduce | flops 12288 | bytes 98304 | tf_op jit(solution)/shard_map/pmax | solution.py:128
  143.3 8.7 %fusion.10 = bf16[2,6,1024,128]{3,2,1,0:T(8,128)(2,1)S(1)} fusion(f32[2,6,4,128]{3,2,1,0:T(4,128)S(1)} %bitcast.167, f32[2,6,510,128]{3,2,1,0:T(8,128)} %fusion.25, f32[2,6,510,128]{3,2,1,0:T(8,128)} %fusion.22, f32[2,6,1024]{2,1,0:T(8,128)S(1)} %get-tuple-element.19, f32[2,6,1024]{2,1,0:T(8,128)S(1)} %get-tuple-element.17, ...), kind=kOutput, calls=%fused_computation.17 | convolution fusion | flops 216268800 | bytes 12902400 | tf_op jit(solution)/shard_map/rhgk,khd->hgrd/dot_general | solution.py:24
  151.9 3.3 %maximum_maximum_fusion = bf16[13,4,4,64,128]{4,3,1,2,0:T(8,128)(2,1)} fusion(bf16[1,4,4,64,12]{4,3,1,2,0:T(8,128)(2,1)S(1)} %copy.131, bf16[1,4,4,64,12]{4,3,1,2,0:T(8,128)(2,1)S(1)} %copy.130, bf16[1,4,4,64,12]{4,3,1,2,0:T(8,128)(2,1)S(1)} %copy.129, bf16[13,128]{1,0:T(8,128)(2,1)S(1)} %pad.4.clone, bf16[12,4,4,64,128]{4,3,2,1,0:T(8,128)(2,1)S(1)} %bitcast.164), kind=kLoop, calls=%fused_computation.25 | loop fusion | flops 17039360 | bytes 6630656 | tf_op jit(solution)/shard_map/concatenate | solution.py:149
  155.2 41.7 %reduce-scatter.2.cloned.1.call-done = bf16[13,256,128]{2,1,0:T(8,128)(2,1)} async-done(((bf16[13,1024,128]{2,1,0:T(8,128)(2,1)}), bf16[13,256,128]{2,1,0:T(8,128)(2,1)}) %reduce-scatter.2.cloned.1.call-update) | async-done | bytes 851984 | tf_op jit(solution)/shard_map/reduce_scatter | solution.py:156
  196.9 1.2 copy.133
  198.2 17.0 %all_to_all.17 = bf16[13,4,64,128]{3,2,0,1:T(8,128)(2,1)S(1)} all-to-all(bf16[13,4,64,128]{3,2,0,1:T(8,128)(2,1)S(1)} %copy.133), channel_id=1, replica_groups=mesh['rep'=16,'wide'=4,'narrow'=4] {'wide'}, dimensions={1} | all-to-all | bytes 1703936 | tf_op jit(solution)/shard_map/all_to_all | solution.py:157
  216.5 13.5 %all_gather.19 = bf16[256,1536]{1,0:T(8,128)(2,1)S(1)} all-gather(bf16[64,1536]{1,0:T(8,128)(2,1)S(1)} %copy_bitcast_fusion.12), channel_id=1, replica_groups=mesh['rep'=16,'wide'=4,'narrow'=4] {'narrow'}, dimensions={0}, use_global_device_ids=true | all-gather | bytes 983040 | tf_op jit(solution)/shard_map/all_gather | solution.py:166
  230.0 1.3 fusion.41
  (68 shorter events, 6.0 us)
Async XLA Ops:
  6.5 223.5 %copy-start = (bf16[1536,384]{1,0:T(8,128)(2,1)S(1)}, bf16[1536,384]{1,0:T(8,128)(2,1)}, u32[]{:S(2)}) copy-start(bf16[1536,384]{1,0:T(8,128)(2,1)} %param.11) | copy-start | bytes 3538948
  6.5 18.9 %copy-start.11 = (f32[1536]{0:T(1024)S(1)}, f32[1536]{0:T(1024)}, u32[]{:S(2)}) copy-start(f32[1536]{0:T(1024)} %param.9) | copy-start | bytes 18436
  6.5 34.2 %all-gather.5.cloned.1.call-start = ((), (), s32[]{:S(2)}) async-start(), calls=%async_computation.5 | async-start | bytes 1966080 | tf_op jit(solution)/shard_map/all_gather | solution.py:74
  7.3 90.5 %all-gather.7.cloned.1.call-start = ((), (), s32[]{:S(2)}) async-start(), calls=%async_computation.6 | async-start | bytes 3342336 | tf_op jit(solution)/shard_map/all_gather | solution.py:80
  25.1 19.3 %copy-start.12 = (s32[2]{0:T(128)S(1)}, s32[2]{0:T(128)}, u32[]{:S(2)}) copy-start(s32[2]{0:T(128)} %param.14) | copy-start | bytes 28
  25.2 19.5 %copy-start.13 = (s32[4]{0:T(128)S(1)}, s32[4]{0:T(128)}, u32[]{:S(2)}) copy-start(s32[4]{0:T(128)} %param.15) | copy-start | bytes 52
  25.2 22.5 %copy-start.5 = (bf16[2,2,512,2,128]{4,3,2,1,0:T(2,128)(2,1)S(1)}, bf16[2,2,512,2,128]{4,3,2,1,0:T(2,128)(2,1)}, u32[]{:S(2)}) copy-start(bf16[2,2,512,2,128]{4,3,2,1,0:T(2,128)(2,1)} %param.12) | copy-start | bytes 3145732
  43.0 0.7 copy-start.6
  53.4 57.5 %all-to-all-start.1 = ((bf16[4,64,128]{2,1,0:T(8,128)(2,1)}), bf16[4,64,128]{2,1,0:T(8,128)(2,1)}, u32[]{:S(2)}, u32[]{:S(2)}) async-start(bf16[4,64,128]{2,1,0:T(8,128)(2,1)} %bitcast.166), calls=%async_computation.1 | async-start | bytes 131072 | tf_op jit(solution)/shard_map/all_to_all | solution.py:87
  57.7 139.3 %reduce-scatter.2.cloned.1.call-start = ((), (), s32[]{:S(2)}) async-start(), calls=%async_computation.4 | async-start | bytes 4259840 | tf_op jit(solution)/shard_map/reduce_scatter | solution.py:156
  97.8 3.1 %copy-start.9 = (bf16[1,1,512,2,128]{4,3,2,1,0:T(2,128)(2,1)S(1)}, bf16[1,1,512,2,128]{4,3,2,1,0:T(2,128)(2,1)}, u32[]{:S(2)}) copy-start(bf16[1,1,512,2,128]{4,3,2,1,0:T(2,128)(2,1)} %get-tuple-element.10) | copy-start | bytes 786436
  100.1 2.7 %copy-start.1 = (bf16[4,256,3,4,128]{4,1,0,3,2:T(8,128)(2,1)}, bf16[4,256,3,4,128]{4,1,0,3,2:T(8,128)(2,1)S(1)}, u32[]{:S(2)}) copy-start(bf16[4,256,3,4,128]{4,1,0,3,2:T(8,128)(2,1)S(1)} %copy.112) | copy-start | bytes 9437188
  102.7 3.6 %copy-start.8 = (bf16[1,1,512,2,128]{4,3,2,1,0:T(2,128)(2,1)S(1)}, bf16[1,1,512,2,128]{4,3,2,1,0:T(2,128)(2,1)}, u32[]{:S(2)}) copy-start(bf16[1,1,512,2,128]{4,3,2,1,0:T(2,128)(2,1)} %get-tuple-element.12) | copy-start | bytes 786436
  106.3 4.5 %copy-start.4 = (pred[1024,64]{0,1:T(8,128)(4,1)S(1)}, pred[1024,64]{0,1:T(8,128)(4,1)}, u32[]{:S(2)}) copy-start(pred[1024,64]{0,1:T(8,128)(4,1)} %compare_and_fusion) | copy-start | bytes 196612
  110.9 5.0 %copy-start.2 = (bf16[4,256,3,4,128]{4,1,0,3,2:T(8,128)(2,1)S(1)}, bf16[4,256,3,4,128]{4,1,0,3,2:T(8,128)(2,1)}, u32[]{:S(2)}) copy-start(bf16[4,256,3,4,128]{4,1,0,3,2:T(8,128)(2,1)} %copy-done.1) | copy-start | bytes 9437188
  114.2 1.7 copy-start.3
  117.9 3.6 %copy-start.7 = (bf16[1,1,512,2,128]{4,3,2,1,0:T(2,128)(2,1)S(1)}, bf16[1,1,512,2,128]{4,3,2,1,0:T(2,128)(2,1)}, u32[]{:S(2)}) copy-start(bf16[1,1,512,2,128]{4,3,2,1,0:T(2,128)(2,1)} %get-tuple-element.9) | copy-start | bytes 786436
  215.1 14.9 %copy-start.10 = (bf16[256,384]{1,0:T(8,128)(2,1)S(1)}, bf16[256,384]{1,0:T(8,128)(2,1)}, u32[]{:S(2)}) copy-start(bf16[256,384]{1,0:T(8,128)(2,1)} %param.8) | copy-start | bytes 589828
Sparse Core Ops, SparseCore 0:
  9.1 31.5 all-gather.4
  44.6 53.1 all-gather.6
  155.3 41.5 reduce-scatter.1
